TPU v7x, 32 devices: a whole 2x2x4 slice. The times are simulated.
32 devices in a mesh: groups: 2 (over x), chan: 16 (over z, y, core).
Axes of the slice: x: 2, y: 2, z: 4, core: 2. Of those that a mesh axis runs over, the one named last changes fastest.
Arguments:
- sky_data: bfloat16 [1024, 512, 2, 256], P('groups', 'chan'), parts along dimension 0, may hold values from -1.1953125 to 1.1953125
- beam_gains: bfloat16 [1024, 512, 256], P('groups', 'chan'), parts along dimension 0, may hold values from 0.099609375 to 1
- mixing: float32 [1024, 4], P(('groups', 'chan')), parts along dimension 0, may hold values from -0.25 to 0.25
- noise_levels: int32 [512], P('chan'), may hold values from 1 to 16
- threshold_levels: int32 [4, 2], replicated, may hold values from 1 to 8
- start_sources: float32 [1024, 4, 256], P(('groups', 'chan')), parts along dimension 0, may hold values from -6 to 6
Outputs:
- sources: float32 [1024, 4, 256], P(('groups', 'chan')), parts along dimension 0
There are 2 independent parts, one for each index of `groups`. A program takes and returns all parts, laid end to end along the dimension named above; an argument that names none is the same for every part. Nothing has to cross between parts.
All inputs are finite; a program needn't handle non-finite values.
Results may differ from a plain program's by a relative error of at most 0.025.
Values may be sent and summed in bfloat16 or wider, within the bound.
No kernel may reach another device: no remote copies, remote signals or barrier semaphores. Data moves between devices by JAX's collectives and lax.ppermute only.
A program may use at most 128 MiB of HBM per device.

v0:
```python
import math

import jax
import jax.numpy as jnp
from jax import lax
from jax.sharding import PartitionSpec as P

ITERS = 2


def padded_2(cells, sides, width):
    for axis, dim in sides:
        count = lax.axis_size(axis)
        ends = count - 1
        head = lax.slice_in_dim(cells, 0, width, axis=dim)
        tail = lax.slice_in_dim(cells, cells.shape[dim] - width, cells.shape[dim], axis=dim)
        cells = jnp.concatenate(
            [
                lax.ppermute(tail, axis, [(i, (i + 1) % count) for i in range(ends)]),
                cells,
                lax.ppermute(head, axis, [((i + 1) % count, i) for i in range(ends)]),
            ],
            axis=dim,
        )
    return cells


def gather_all(strip, axis):
    count = lax.axis_size(axis)
    copies = jnp.broadcast_to(strip[None], (count,) + strip.shape)
    joined = lax.all_to_all(copies, axis, 0, 0, tiled=True)
    return joined.reshape((count * strip.shape[0],) + strip.shape[1:])


def gather_rows(strip, axis):
    count = lax.axis_size(axis)
    bits = count.bit_length() - 1
    assert 1 << bits == count
    own = lax.axis_index(axis)
    joined = strip
    for depth, bit in enumerate(reversed(range(bits))):
        partner = lax.ppermute(joined, axis, [(i, i ^ (1 << bit)) for i in range(count)])
        upper = ((own >> bit) & 1) == 1
        low = jnp.where(upper, partner, joined)
        high = jnp.where(upper, joined, partner)
        joined = jnp.stack([low, high], axis=depth)
    return joined.reshape((count * strip.shape[0],) + strip.shape[1:])


def sum_rows(values, axis):
    count = lax.axis_size(axis)
    half = count // 2
    parity = lax.axis_index(axis) % 2
    strip = values.shape[0] // count
    pairs = values.reshape((half, 2, strip) + values.shape[1:])
    even = pairs[:, 0]
    odd = pairs[:, 1]
    keep = jnp.where(parity == 1, odd, even)
    send = jnp.where(parity == 1, even, odd)
    moved = lax.ppermute(
        send.astype(jnp.bfloat16), axis, [(i, i ^ 1) for i in range(count)]
    )
    chip_sum = (keep + moved.astype(jnp.float32)).astype(jnp.bfloat16)
    groups = [list(range(p, count, 2)) for p in range(2)]
    received = lax.all_to_all(chip_sum, axis, 0, 0, tiled=True, axis_index_groups=groups)
    return received.astype(jnp.float32).sum(axis=0)


def dft_tables(length):
    positions = jnp.arange(length, dtype=jnp.int32)
    angles = (positions[:, None] * positions[None, :] % length).astype(jnp.float32) * (
        2.0 * math.pi / length
    )
    norm_factor = 1.0 / math.sqrt(length)
    return (
        (jnp.cos(angles) * norm_factor).astype(jnp.bfloat16),
        (-jnp.sin(angles) * norm_factor).astype(jnp.bfloat16),
    )


def column_part(rounded, col_cat):
    row_count, source_count, col_count = rounded.shape
    product = jnp.dot(
        rounded.reshape(row_count * source_count, col_count),
        col_cat,
        preferred_element_type=jnp.float32,
    )
    return product.astype(jnp.bfloat16).reshape(row_count, source_count * 2 * col_count)


def combine_forward(real_prod, imag_prod, source_count, col_count):
    real_prod = real_prod.reshape(real_prod.shape[0], source_count, 2, col_count)
    imag_prod = imag_prod.reshape(imag_prod.shape[0], source_count, 2, col_count)
    real_out = real_prod[:, :, 0] - imag_prod[:, :, 1]
    imag_out = real_prod[:, :, 1] + imag_prod[:, :, 0]
    return jnp.stack([real_out, imag_out], axis=2)


def inverse_rows(row_real, row_imag, packed_grad, col_back, source_count, col_count):
    real_prod = jnp.dot(row_real, packed_grad, preferred_element_type=jnp.float32)
    imag_prod = jnp.dot(row_imag, packed_grad, preferred_element_type=jnp.float32)
    real_prod = real_prod.reshape(real_prod.shape[0], source_count, 2, col_count)
    imag_prod = imag_prod.reshape(imag_prod.shape[0], source_count, 2, col_count)
    real_out = real_prod[:, :, 0] + imag_prod[:, :, 1]
    imag_out = real_prod[:, :, 1] - imag_prod[:, :, 0]
    joined = jnp.concatenate([real_out, imag_out], axis=-1).astype(jnp.bfloat16)
    result = jnp.dot(
        joined.reshape(-1, 2 * col_count), col_back, preferred_element_type=jnp.float32
    )
    return result.reshape(real_prod.shape[0], source_count, col_count)


def block_gradient(fourier, data_block, beam_block, mix_block, level_block):
    predicted = jnp.einsum("ct,ktzl->kczl", mix_block, fourier)
    beam_gain = beam_block.astype(jnp.float32)[:, :, None, :]
    residual = data_block.astype(jnp.float32) - beam_gain * predicted
    weight = level_block.astype(jnp.float32) * 0.25
    weighted_mix = mix_block * weight[:, None]
    summed = jnp.einsum("cs,kczl->kszl", weighted_mix, beam_gain * residual)
    return summed.astype(jnp.bfloat16)


def smooth_rows(padded, spacing, row_count):
    return (
        padded[0:row_count]
        + 2.0 * padded[spacing : spacing + row_count]
        + padded[2 * spacing : 2 * spacing + row_count]
    ) * 0.25


def smooth_cols(values, spacing):
    padded = jnp.pad(values, ((0, 0), (0, 0), (spacing, spacing)))
    return (
        padded[..., : -2 * spacing]
        + 2.0 * padded[..., spacing:-spacing]
        + padded[..., 2 * spacing :]
    ) * 0.25


def shrink(values, bound_value):
    return values - jnp.clip(values, -bound_value, bound_value)


def combine_scales(updated, smooth_one, coarse, fine_bound, coarse_bound):
    return (
        coarse
        + shrink(smooth_one - coarse, coarse_bound)
        + shrink(updated - smooth_one, fine_bound)
    )


def body(sky_data, beam_gains, mixing, noise_levels, threshold_levels, start_sources):
    strip_rows, source_count, col_count = start_sources.shape
    full_rows = strip_rows * lax.axis_size("chan")
    row_real, row_imag = dft_tables(full_rows)
    col_real, col_imag = dft_tables(col_count)
    col_cat = jnp.concatenate([col_real, col_imag], axis=1)
    col_back = jnp.concatenate([col_real, col_imag], axis=0)
    bounds = threshold_levels.astype(jnp.float32) * 0.05
    fine_bound = bounds[:, 0][:, None]
    coarse_bound = bounds[:, 1][:, None]
    first_row = lax.axis_index("chan") * strip_rows
    sources = start_sources
    for iteration in range(ITERS):
        rounded = sources.astype(jnp.bfloat16)
        gather = gather_all if iteration == 0 else gather_rows
        gathered = gather(rounded, "chan")
        by_source = jnp.transpose(gathered, (1, 0, 2))
        packed = jnp.dot(
            by_source.reshape(-1, col_count), col_cat, preferred_element_type=jnp.float32
        ).astype(jnp.bfloat16).reshape(source_count, full_rows, 2, col_count)
        real_prod = jnp.einsum("kr,srzl->kszl", row_real, packed, preferred_element_type=jnp.float32)
        imag_prod = jnp.einsum("kr,srzl->kszl", row_imag, packed, preferred_element_type=jnp.float32)
        fourier = jnp.stack(
            [real_prod[:, :, 0] - imag_prod[:, :, 1], real_prod[:, :, 1] + imag_prod[:, :, 0]],
            axis=2,
        )
        grad_local = block_gradient(fourier, sky_data, beam_gains, mixing, noise_levels)
        packed_grad = grad_local.reshape(full_rows, source_count * 2 * col_count)
        gradient = sum_rows(
            inverse_rows(row_real, row_imag, packed_grad, col_back, source_count, col_count),
            "chan",
        )
        updated = sources + gradient
        wide_pad = padded_2(updated, (("chan", 0),), 3)
        smooth_wide = smooth_cols(smooth_rows(wide_pad, 1, strip_rows + 4), 1)
        inside = (first_row - 2 + jnp.arange(strip_rows + 4) >= 0) & (
            first_row - 2 + jnp.arange(strip_rows + 4) < full_rows
        )
        smooth_wide = jnp.where(inside[:, None, None], smooth_wide, 0.0)
        smooth_one = smooth_wide[2 : 2 + strip_rows]
        coarse = smooth_cols(smooth_rows(smooth_wide, 2, strip_rows), 2)
        sources = combine_scales(updated, smooth_one, coarse, fine_bound, coarse_bound)
    return sources


def solution(mesh):
    return jax.shard_map(
        body,
        mesh=mesh,
        in_specs=(
            P("groups", "chan", None, None),
            P("groups", "chan", None),
            P(("groups", "chan"), None),
            P("chan"),
            P(),
            P(("groups", "chan"), None, None),
        ),
        out_specs=P(("groups", "chan"), None, None),
        check_vma=False,
    )
```

profile of v0, /device:TPU:1, one launch (start us, length us, event | category | flops | bytes accessed | tf_op | source)
XLA Modules:
  0.0 223.1 jit_solution(1778259923165652414)
XLA Ops:
  2.1 7.3 %all-to-all-start = ((bf16[16,32,4,256]{3,1,2,0:T(8,128)(2,1)}), bf16[16,32,4,256]{3,1,2,0:T(8,128)(2,1)S(1)}, u32[]{:S(2)}, u32[]{:S(2)}) async-start(bf16[16,32,4,256]{3,1,2,0:T(8,128)(2,1)} %broadcast_in_dim.43), calls=%async_computation | async-start | bytes 2097152 | tf_op jit(solution)/shard_map/all_to_all | solution.py:31
  9.4 11.3 %convert_element_type.140 = f32[512,32,256]{2,1,0:T(8,128)} convert(bf16[512,32,256]{2,1,0:T(8,128)(2,1)} %param.7) | non-fusion elementwise | flops 4194304 | bytes 25165824 | tf_op jit(solution)/shard_map/convert_element_type | solution.py:115
  21.9 10.7 %all-to-all-done = bf16[16,32,4,256]{3,1,2,0:T(8,128)(2,1)S(1)} async-done(((bf16[16,32,4,256]{3,1,2,0:T(8,128)(2,1)}), bf16[16,32,4,256]{3,1,2,0:T(8,128)(2,1)S(1)}, u32[]{:S(2)}, u32[]{:S(2)}) %all-to-all-start) | async-done | bytes 1048608 | tf_op jit(solution)/shard_map/all_to_all | solution.py:31
  36.2 3.2 %copy.51 = bf16[4,512,2,256]{3,1,2,0:T(8,128)(2,1)S(1)} copy(bf16[4,512,2,256]{1,0,3,2:T(4,128)(2,1)} %reshape.90) | data formatting | bytes 4194304 | tf_op jit(solution)/shard_map/reshape | solution.py:171
  39.4 4.9 %fusion.64 = f32[512,4,2,256]{3,0,2,1:T(8,128)S(1)} fusion(bf16[4,512,2,256]{3,1,2,0:T(8,128)(2,1)S(1)} %copy.51), kind=kOutput, calls=%fused_computation.82 | convolution fusion | flops 1078198272 | bytes 6291456 | tf_op jit(solution)/shard_map/kr,srzl->kszl/dot_general | solution.py:173
  44.3 4.9 %fusion.69 = f32[512,4,2,256]{3,0,2,1:T(8,128)S(1)} fusion(bf16[4,512,2,256]{3,1,2,0:T(8,128)(2,1)S(1)} %copy.51), kind=kOutput, calls=%fused_computation.83 | convolution fusion | flops 1077936128 | bytes 6291456 | tf_op jit(solution)/shard_map/kr,srzl->kszl/dot_general | solution.py:172
  50.7 21.8 %convert_bitcast_fusion.1 = bf16[512,4,2,256]{3,1,2,0:T(4,128)(2,1)} fusion(f32[512,32,256]{2,1,0:T(8,128)} %convert_element_type.140, bf16[512,32,2,256]{3,2,1,0:T(2,128)(2,1)} %param.6, bf16[512,4,2,256]{3,0,2,1:T(8,128)(2,1)S(1)} %pad_maximum_fusion, f32[32,4]{0,1:T(4,128)S(1)} %copy-done.3, f32[32]{0:T(128)S(1)} %convert_multiply_fusion.1), kind=kOutput, calls=%fused_computation.48 | convolution fusion | flops 176160896 | bytes 37749376 | tf_op jit(solution)/shard_map/cs,kczl->kszl/dot_general | solution.py:119
  72.5 3.0 %copy.54 = bf16[512,4,2,256]{0,3,2,1:T(8,128)(2,1)S(1)} copy(bf16[512,4,2,256]{3,1,2,0:T(4,128)(2,1)} %convert_bitcast_fusion.1) | data formatting | bytes 4194304 | tf_op jit(solution)/shard_map/convert_element_type | solution.py:120
  75.5 4.9 %fusion.31 = f32[512,4,2,256]{3,0,2,1:T(8,128)S(1)} fusion(bf16[512,4,2,256]{0,3,2,1:T(8,128)(2,1)S(1)} %copy.54), kind=kOutput, calls=%fused_computation.43 | convolution fusion | flops 1078198272 | bytes 6291456 | tf_op jit(solution)/shard_map/dot_general | solution.py:101
  80.4 4.9 %fusion.33 = f32[512,4,2,256]{3,0,2,1:T(8,128)S(1)} fusion(bf16[512,4,2,256]{0,3,2,1:T(8,128)(2,1)S(1)} %copy.54), kind=kOutput, calls=%fused_computation.45 | convolution fusion | flops 1077936128 | bytes 6291456 | tf_op jit(solution)/shard_map/dot_general | solution.py:100
  90.2 6.2 %all-to-all-start.1 = ((bf16[8,32,4,256]{3,1,2,0:T(8,128)(2,1)}), bf16[8,32,4,256]{3,1,2,0:T(8,128)(2,1)S(1)}, u32[]{:S(2)}, u32[]{:S(2)}) async-start(bf16[8,32,4,256]{3,1,2,0:T(8,128)(2,1)} %fusion.52), calls=%async_computation.1 | async-start | bytes 1048576 | tf_op jit(solution)/shard_map/all_to_all | solution.py:65
  96.4 13.8 %all-to-all-done.1 = bf16[8,32,4,256]{3,1,2,0:T(8,128)(2,1)S(1)} async-done(((bf16[8,32,4,256]{3,1,2,0:T(8,128)(2,1)}), bf16[8,32,4,256]{3,1,2,0:T(8,128)(2,1)S(1)}, u32[]{:S(2)}, u32[]{:S(2)}) %all-to-all-start.1) | async-done | bytes 524320 | tf_op jit(solution)/shard_map/all_to_all | solution.py:65
  110.3 4.6 %collective-permute-start.1 = (f32[3,4,256]{2,0,1:T(4,128)S(1)}, f32[3,4,256]{2,0,1:T(4,128)S(1)}, u32[]{:S(2)}, u32[]{:S(2)}) collective-permute-start(f32[3,4,256]{2,0,1:T(4,128)S(1)} %get-tuple-element.25), channel_id=1, source_target_pairs={{0,1},{1,2},{2,3},{3,4},{4,5},{5,6},{6,7},{7,8},{8,9},{9,10},{10,1... | collective-permute-start | bytes 36872 | tf_op jit(solution)/shard_map/ppermute | solution.py:19
  120.5 4.7 %collective-permute-done.3 = bf16[32,4,256]{2,0,1:T(8,128)(2,1)S(1)} collective-permute-done((bf16[32,4,256]{2,0,1:T(8,128)(2,1)S(1)}, bf16[32,4,256]{2,0,1:T(8,128)(2,1)S(1)}, u32[]{:S(2)}, u32[]{:S(2)}) %collective-permute-start.3) | collective-permute-done | bytes 65568 | tf_op jit(solution)/shard_map/ppermute | solution.py:42
  125.4 4.9 %collective-permute-done.4 = bf16[2,32,4,256]{3,1,0,2:T(8,128)(2,1)S(1)} collective-permute-done((bf16[2,32,4,256]{3,1,0,2:T(8,128)(2,1)S(1)}, bf16[2,32,4,256]{3,1,0,2:T(8,128)(2,1)S(1)}, u32[]{:S(2)}, u32[]{:S(2)}) %collective-permute-start.4) | collective-permute-done | bytes 131104 | tf_op jit(solution)/shard_map/ppermute | solution.py:42
  131.5 6.1 %collective-permute-done.5 = bf16[2,2,32,4,256]{4,2,1,0,3:T(8,128)(2,1)S(1)} collective-permute-done((bf16[2,2,32,4,256]{4,2,1,0,3:T(8,128)(2,1)S(1)}, bf16[2,2,32,4,256]{4,2,1,0,3:T(8,128)(2,1)S(1)}, u32[]{:S(2)}, u32[]{:S(2)}) %collective-permute-start.5) | collective-permute-done | bytes 262176 | tf_op jit(solution)/shard_map/ppermute | solution.py:42
  143.8 6.7 %fusion.43 = f32[512,4,2,256]{3,0,2,1:T(8,128)S(1)} fusion(bf16[4,512,2,256]{3,2,1,0:T(2,128)(2,1)} %reshape.94), kind=kOutput, calls=%fused_computation.49 | convolution fusion | flops 1078198272 | bytes 6291456 | tf_op jit(solution)/shard_map/kr,srzl->kszl/dot_general | solution.py:173
  150.5 4.9 %fusion.45 = f32[512,4,2,256]{3,0,2,1:T(8,128)S(1)} fusion(bf16[4,512,2,256]{3,2,1,0:T(2,128)(2,1)S(1)} %copy-done), kind=kOutput, calls=%fused_computation.51 | convolution fusion | flops 1077936128 | bytes 6291456 | tf_op jit(solution)/shard_map/kr,srzl->kszl/dot_general | solution.py:172
  156.5 21.2 %convert_bitcast_fusion = bf16[512,4,2,256]{3,1,2,0:T(4,128)(2,1)} fusion(f32[512,32,256]{2,1,0:T(8,128)} %convert_element_type.140, bf16[512,32,2,256]{3,2,1,0:T(2,128)(2,1)} %param.6, bf16[512,4,2,256]{3,0,2,1:T(8,128)(2,1)S(1)} %pad_maximum_fusion.1, f32[32,4]{0,1:T(4,128)S(1)} %copy-done.3, f32[32]{0:T(128)S(1)} %convert_multiply_fusion.1), kind=kOutput, calls=%fused_computation.47 | convolution fusion | flops 176160896 | bytes 37749376 | tf_op jit(solution)/shard_map/cs,kczl->kszl/dot_general | solution.py:119
  180.7 4.9 %fusion.25 = f32[512,4,2,256]{3,0,2,1:T(8,128)S(1)} fusion(bf16[512,4,2,256]{0,3,2,1:T(8,128)(2,1)S(1)} %copy.69), kind=kOutput, calls=%fused_computation.37 | convolution fusion | flops 1078198272 | bytes 6291456 | tf_op jit(solution)/shard_map/dot_general | solution.py:101
  185.6 4.9 %fusion.27 = f32[512,4,2,256]{3,0,2,1:T(8,128)S(1)} fusion(bf16[512,4,2,256]{0,3,2,1:T(8,128)(2,1)S(1)} %copy.69), kind=kOutput, calls=%fused_computation.39 | convolution fusion | flops 1077936128 | bytes 6291456 | tf_op jit(solution)/shard_map/dot_general | solution.py:100
  194.6 17.2 %all_to_all.15 = bf16[8,32,4,256]{3,1,2,0:T(8,128)(2,1)S(1)} all-to-all(bf16[8,32,4,256]{3,1,2,0:T(8,128)(2,1)S(1)} %fusion.53), channel_id=1, replica_groups={{0,2,4,6,8,10,12,14},{1,3,5,7,9,11,13,15},{16,18,20,22,24,26,28,30},{17..., dimensions={0} | all-to-all | bytes 1048576 | tf_op jit(solution)/shard_map/all_to_all | solution.py:65
  211.9 4.7 %collective-permute-start.8 = (f32[3,4,256]{2,0,1:T(4,128)S(1)}, f32[3,4,256]{2,0,1:T(4,128)S(1)}, u32[]{:S(2)}, u32[]{:S(2)}) collective-permute-start(f32[3,4,256]{2,0,1:T(4,128)S(1)} %get-tuple-element.21), channel_id=1, source_target_pairs={{0,1},{1,2},{2,3},{3,4},{4,5},{5,6},{6,7},{7,8},{8,9},{9,10},{10,1... | collective-permute-start | bytes 36872 | tf_op jit(solution)/shard_map/ppermute | solution.py:19
  218.5 3.1 %collective-permute-done.9 = f32[3,4,256]{2,0,1:T(4,128)S(1)} collective-permute-done((f32[3,4,256]{2,0,1:T(4,128)S(1)}, f32[3,4,256]{2,0,1:T(4,128)S(1)}, u32[]{:S(2)}, u32[]{:S(2)}) %collective-permute-start.9) | collective-permute-done | bytes 12320 | tf_op jit(solution)/shard_map/ppermute | solution.py:21
  (75 shorter events, 37.7 us)
Async XLA Ops:
  2.1 30.5 %all-to-all-start = ((bf16[16,32,4,256]{3,1,2,0:T(8,128)(2,1)}), bf16[16,32,4,256]{3,1,2,0:T(8,128)(2,1)S(1)}, u32[]{:S(2)}, u32[]{:S(2)}) async-start(bf16[16,32,4,256]{3,1,2,0:T(8,128)(2,1)} %broadcast_in_dim.43), calls=%async_computation | async-start | bytes 2097152 | tf_op jit(solution)/shard_map/all_to_all | solution.py:31
  9.4 12.4 %copy-start.4 = (s32[32]{0:T(128)S(1)}, s32[32]{0:T(128)}, u32[]{:S(2)}) copy-start(s32[32]{0:T(128)} %param.9) | copy-start | bytes 388
  50.1 0.7 copy-start.3
  87.1 9.3 %copy-start.2 = (s32[4,2]{0,1:T(2,128)S(1)}, s32[4,2]{0,1:T(2,128)}, u32[]{:S(2)}) copy-start(s32[4,2]{0,1:T(2,128)} %param.10) | copy-start | bytes 100
  87.1 23.1 %copy-start.1 = (f32[32,4,256]{2,1,0:T(4,128)S(1)}, f32[32,4,256]{2,1,0:T(4,128)}, u32[]{:S(2)}) copy-start(f32[32,4,256]{2,1,0:T(4,128)} %param.11) | copy-start | bytes 393220
  87.1 2.0 collective-permute-start
  90.2 20.0 %all-to-all-start.1 = ((bf16[8,32,4,256]{3,1,2,0:T(8,128)(2,1)}), bf16[8,32,4,256]{3,1,2,0:T(8,128)(2,1)S(1)}, u32[]{:S(2)}, u32[]{:S(2)}) async-start(bf16[8,32,4,256]{3,1,2,0:T(8,128)(2,1)} %fusion.52), calls=%async_computation.1 | async-start | bytes 1048576 | tf_op jit(solution)/shard_map/all_to_all | solution.py:65
  110.3 6.7 %collective-permute-start.1 = (f32[3,4,256]{2,0,1:T(4,128)S(1)}, f32[3,4,256]{2,0,1:T(4,128)S(1)}, u32[]{:S(2)}, u32[]{:S(2)}) collective-permute-start(f32[3,4,256]{2,0,1:T(4,128)S(1)} %get-tuple-element.25), channel_id=1, source_target_pairs={{0,1},{1,2},{2,3},{3,4},{4,5},{5,6},{6,7},{7,8},{8,9},{9,10},{10,1... | collective-permute-start | bytes 36872 | tf_op jit(solution)/shard_map/ppermute | solution.py:19
  114.9 5.1 %collective-permute-start.2 = (f32[3,4,256]{2,0,1:T(4,128)S(1)}, f32[3,4,256]{2,0,1:T(4,128)S(1)}, u32[]{:S(2)}, u32[]{:S(2)}) collective-permute-start(f32[3,4,256]{2,0,1:T(4,128)S(1)} %get-tuple-element.26), channel_id=1, source_target_pairs={{1,0},{2,1},{3,2},{4,3},{5,4},{6,5},{7,6},{8,7},{9,8},{10,9},{11,1... | collective-permute-start | bytes 36872 | tf_op jit(solution)/shard_map/ppermute | solution.py:21
  120.5 4.8 %collective-permute-start.3 = (bf16[32,4,256]{2,0,1:T(8,128)(2,1)S(1)}, bf16[32,4,256]{2,0,1:T(8,128)(2,1)S(1)}, u32[]{:S(2)}, u32[]{:S(2)}) collective-permute-start(bf16[32,4,256]{2,0,1:T(8,128)(2,1)S(1)} %get-tuple-element.5), channel_id=1, source_target_pairs={{0,8},{1,9},{2,10},{3,11},{4,12},{5,13},{6,14},{7,15},{8,0},{9,1},... | collective-permute-start | bytes 196616 | tf_op jit(solution)/shard_map/ppermute | solution.py:42
  125.3 5.0 %collective-permute-start.4 = (bf16[2,32,4,256]{3,1,0,2:T(8,128)(2,1)S(1)}, bf16[2,32,4,256]{3,1,0,2:T(8,128)(2,1)S(1)}, u32[]{:S(2)}, u32[]{:S(2)}) collective-permute-start(bf16[2,32,4,256]{3,1,0,2:T(8,128)(2,1)S(1)} %pad_maximum_fusion.15), channel_id=1, source_target_pairs={{0,4},{1,5},{2,6},{3,7},{4,0},{5,1},{6,2},{7,3},{8,12},{9,13},{10,... | collective-permute-start | bytes 393224 | tf_op jit(solution)/shard_map/ppermute | solution.py:42
  130.3 7.3 %collective-permute-start.5 = (bf16[2,2,32,4,256]{4,2,1,0,3:T(8,128)(2,1)S(1)}, bf16[2,2,32,4,256]{4,2,1,0,3:T(8,128)(2,1)S(1)}, u32[]{:S(2)}, u32[]{:S(2)}) collective-permute-start(bf16[2,2,32,4,256]{4,2,1,0,3:T(8,128)(2,1)S(1)} %pad_maximum_fusion.8), channel_id=1, source_target_pairs={{0,2},{1,3},{2,0},{3,1},{4,6},{5,7},{6,4},{7,5},{8,10},{9,11},{10,... | collective-permute-start | bytes 786440 | tf_op jit(solution)/shard_map/ppermute | solution.py:42
  137.7 3.1 %collective-permute-start.6 = (bf16[2,2,2,32,4,256]{5,3,2,1,0,4:T(8,128)(2,1)S(1)}, bf16[2,2,2,32,4,256]{5,3,2,1,0,4:T(8,128)(2,1)S(1)}, u32[]{:S(2)}, u32[]{:S(2)}) collective-permute-start(bf16[2,2,2,32,4,256]{5,3,2,1,0,4:T(8,128)(2,1)S(1)} %pad_maximum_fusion.5), channel_id=1, source_target_pairs={{0,1},{1,0},{2,3},{3,2},{4,5},{5,4},{6,7},{7,6},{8,9},{9,8},{10,11... | collective-permute-start | bytes 1572872 | tf_op jit(solution)/shard_map/ppermute | solution.py:42
  143.8 6.7 %copy-start = (bf16[4,512,2,256]{3,2,1,0:T(2,128)(2,1)S(1)}, bf16[4,512,2,256]{3,2,1,0:T(2,128)(2,1)}, u32[]{:S(2)}) copy-start(bf16[4,512,2,256]{3,2,1,0:T(2,128)(2,1)} %reshape.94) | copy-start | bytes 6291460
  192.3 2.0 collective-permute-start.7
  211.9 6.7 %collective-permute-start.8 = (f32[3,4,256]{2,0,1:T(4,128)S(1)}, f32[3,4,256]{2,0,1:T(4,128)S(1)}, u32[]{:S(2)}, u32[]{:S(2)}) collective-permute-start(f32[3,4,256]{2,0,1:T(4,128)S(1)} %get-tuple-element.21), channel_id=1, source_target_pairs={{0,1},{1,2},{2,3},{3,4},{4,5},{5,6},{6,7},{7,8},{8,9},{9,10},{10,1... | collective-permute-start | bytes 36872 | tf_op jit(solution)/shard_map/ppermute | solution.py:19
  216.6 5.1 %collective-permute-start.9 = (f32[3,4,256]{2,0,1:T(4,128)S(1)}, f32[3,4,256]{2,0,1:T(4,128)S(1)}, u32[]{:S(2)}, u32[]{:S(2)}) collective-permute-start(f32[3,4,256]{2,0,1:T(4,128)S(1)} %get-tuple-element.22), channel_id=1, source_target_pairs={{1,0},{2,1},{3,2},{4,3},{5,4},{6,5},{7,6},{8,7},{9,8},{10,9},{11,1... | collective-permute-start | bytes 36872 | tf_op jit(solution)/shard_map/ppermute | solution.py:21
where the time goes:
time: 227 us; the launch traced here: 223 us
  matrix products  86.8 us (38%)
  waiting for transfers between devices  51.2 us (23%)
  starting transfers between devices  30.3 us (13%)
  other arithmetic  20.6 us (9%)
  blocking collectives  17.2 us (8%)
  local copies, waits for them, and re-layouts  16.4 us (7%)
    dot_general x2, matrix products, block_gradient(): summed = jnp.einsum('cs,kczl->kszl', weighted_mix, beam_gain * residual)  43 us
    ppermute x4, waiting for transfers between devices, gather_rows(): lax.ppermute(joined, axis, [(i, i ^ 1 << bit) for i in range(count)])  17.2 us
    all_to_all x1, blocking collectives, sum_rows(): lax.all_to_all(chip_sum, axis, 0, 0, tiled=True, axis_index_groups=groups)  17.2 us
    all_to_all x1, waiting for transfers between devices, sum_rows(): lax.all_to_all(chip_sum, axis, 0, 0, tiled=True, axis_index_groups=groups)  13.8 us
    dot_general x2, matrix products, body(): jnp.einsum('kr,srzl->kszl', row_imag, packed, preferred_element_type=jnp....  11.6 us
    convert_element_type x1, other arithmetic, block_gradient(): beam_gain = beam_block.astype(jnp.float32)[:, :, None, :]  11.3 us
    all_to_all x1, waiting for transfers between devices, gather_all(): joined = lax.all_to_all(copies, axis, 0, 0, tiled=True)  10.7 us
    dot_general x2, matrix products, body(): jnp.einsum('kr,srzl->kszl', row_real, packed, preferred_element_type=jnp....  9.81 us
  transfers between devices with their start and end apart: 12, of which 10 were waited for; matrix products, arithmetic and copies ran while one was open for 6% of the time, Pallas kernels for 0%

commit v1 on v0

--- a/solution.py
+++ b/solution.py
@@ -97,10 +97,8 @@
 
 
 def inverse_rows(row_real, row_imag, packed_grad, col_back, source_count, col_count):
-    real_prod = jnp.dot(row_real, packed_grad, preferred_element_type=jnp.float32)
-    imag_prod = jnp.dot(row_imag, packed_grad, preferred_element_type=jnp.float32)
-    real_prod = real_prod.reshape(real_prod.shape[0], source_count, 2, col_count)
-    imag_prod = imag_prod.reshape(imag_prod.shape[0], source_count, 2, col_count)
+    real_prod = jnp.einsum("rk,kszl->rszl", row_real, packed_grad, preferred_element_type=jnp.float32)
+    imag_prod = jnp.einsum("rk,kszl->rszl", row_imag, packed_grad, preferred_element_type=jnp.float32)
     real_out = real_prod[:, :, 0] + imag_prod[:, :, 1]
     imag_out = real_prod[:, :, 1] - imag_prod[:, :, 0]
     joined = jnp.concatenate([real_out, imag_out], axis=-1).astype(jnp.bfloat16)
@@ -176,7 +174,7 @@
             axis=2,
         )
         grad_local = block_gradient(fourier, sky_data, beam_gains, mixing, noise_levels)
-        packed_grad = grad_local.reshape(full_rows, source_count * 2 * col_count)
+        packed_grad = grad_local
         gradient = sum_rows(
             inverse_rows(row_real, row_imag, packed_grad, col_back, source_count, col_count),
             "chan",

time: 227 us -> 226 us (level)
  local copies, waits for them, and re-layouts: 16.4 us -> 10.5 us
  matrix products: 86.8 us -> 91 us
    convert_element_type x2 -> x0, local copies, waits for them, and re-layouts: 5.93 us -> none  [block_gradient(): return summed.astype(jnp.bfloat16)]
    dot_general x4, matrix products: 19.6 us -> 23.8 us  [the longest x2 13.7 us: inverse_rows(): jnp.einsum('rk,kszl->rszl', row_imag, packed_grad, preferred_element_type...]
where the time goes in v1:
time: 226 us; the launch traced here: 222 us
  matrix products  91 us (40%)
  waiting for transfers between devices  51.4 us (23%)
  starting transfers between devices  30.3 us (13%)
  other arithmetic  20.6 us (9%)
  blocking collectives  17.2 us (8%)
  local copies, waits for them, and re-layouts  10.5 us (5%)
    dot_general x2, matrix products, block_gradient(): summed = jnp.einsum('cs,kczl->kszl', weighted_mix, beam_gain * residual)  42.9 us
    ppermute x4, waiting for transfers between devices, gather_rows(): lax.ppermute(joined, axis, [(i, i ^ 1 << bit) for i in range(count)])  17.2 us
    all_to_all x1, blocking collectives, sum_rows(): lax.all_to_all(chip_sum, axis, 0, 0, tiled=True, axis_index_groups=groups)  17.2 us
    all_to_all x1, waiting for transfers between devices, sum_rows(): lax.all_to_all(chip_sum, axis, 0, 0, tiled=True, axis_index_groups=groups)  13.8 us
    dot_general x2, matrix products, inverse_rows(): jnp.einsum('rk,kszl->rszl', row_imag, packed_grad, preferred_element_type...  13.7 us
    dot_general x2, matrix products, body(): jnp.einsum('kr,srzl->kszl', row_imag, packed, preferred_element_type=jnp....  11.6 us
    convert_element_type x1, other arithmetic, block_gradient(): beam_gain = beam_block.astype(jnp.float32)[:, :, None, :]  11.3 us
    all_to_all x1, waiting for transfers between devices, gather_all(): joined = lax.all_to_all(copies, axis, 0, 0, tiled=True)  10.7 us
  transfers between devices with their start and end apart: 12, of which 10 were waited for; matrix products, arithmetic and copies ran while one was open for 6% of the time, Pallas kernels for 0%

profile of v1, /device:TPU:1, one launch (start us, length us, event | category | flops | bytes accessed | tf_op | source)
XLA Modules:
  0.0 221.5 jit_solution(3609327893311804393)
XLA Ops:
  2.1 7.3 %all-to-all-start = ((bf16[16,32,4,256]{3,1,2,0:T(8,128)(2,1)}), bf16[16,32,4,256]{3,1,2,0:T(8,128)(2,1)S(1)}, u32[]{:S(2)}, u32[]{:S(2)}) async-start(bf16[16,32,4,256]{3,1,2,0:T(8,128)(2,1)} %broadcast_in_dim.43), calls=%async_computation | async-start | bytes 2097152 | tf_op jit(solution)/shard_map/all_to_all | solution.py:31
  9.4 11.3 %convert_element_type.140 = f32[512,32,256]{2,1,0:T(8,128)} convert(bf16[512,32,256]{2,1,0:T(8,128)(2,1)} %param.7) | non-fusion elementwise | flops 4194304 | bytes 25165824 | tf_op jit(solution)/shard_map/convert_element_type | solution.py:113
  21.9 10.7 %all-to-all-done = bf16[16,32,4,256]{3,1,2,0:T(8,128)(2,1)S(1)} async-done(((bf16[16,32,4,256]{3,1,2,0:T(8,128)(2,1)}), bf16[16,32,4,256]{3,1,2,0:T(8,128)(2,1)S(1)}, u32[]{:S(2)}, u32[]{:S(2)}) %all-to-all-start) | async-done | bytes 1048608 | tf_op jit(solution)/shard_map/all_to_all | solution.py:31
  36.2 3.2 %copy.57 = bf16[4,512,2,256]{3,1,2,0:T(8,128)(2,1)S(1)} copy(bf16[4,512,2,256]{1,0,3,2:T(4,128)(2,1)} %reshape.76) | data formatting | bytes 4194304 | tf_op jit(solution)/shard_map/reshape | solution.py:169
  39.4 4.9 %fusion.64 = f32[512,4,2,256]{3,0,2,1:T(8,128)S(1)} fusion(bf16[4,512,2,256]{3,1,2,0:T(8,128)(2,1)S(1)} %copy.57), kind=kOutput, calls=%fused_computation.82 | convolution fusion | flops 1078198272 | bytes 6291456 | tf_op jit(solution)/shard_map/kr,srzl->kszl/dot_general | solution.py:171
  44.3 4.9 %fusion.69 = f32[512,4,2,256]{3,0,2,1:T(8,128)S(1)} fusion(bf16[4,512,2,256]{3,1,2,0:T(8,128)(2,1)S(1)} %copy.57), kind=kOutput, calls=%fused_computation.83 | convolution fusion | flops 1077936128 | bytes 6291456 | tf_op jit(solution)/shard_map/kr,srzl->kszl/dot_general | solution.py:170
  50.7 21.7 %convert_bitcast_fusion.1 = bf16[512,4,2,256]{3,1,2,0:T(4,128)(2,1)} fusion(f32[512,32,256]{2,1,0:T(8,128)} %convert_element_type.140, bf16[512,32,2,256]{3,2,1,0:T(2,128)(2,1)} %param.6, bf16[512,4,2,256]{3,0,2,1:T(8,128)(2,1)S(1)} %pad_maximum_fusion, f32[32,4]{0,1:T(4,128)S(1)} %copy-done.3, f32[32]{0:T(128)S(1)} %convert_multiply_fusion.1), kind=kOutput, calls=%fused_computation.40 | convolution fusion | flops 176160896 | bytes 37749376 | tf_op jit(solution)/shard_map/cs,kczl->kszl/dot_general | solution.py:117
  72.4 6.9 %fusion.43 = f32[512,4,2,256]{3,0,2,1:T(8,128)S(1)} fusion(bf16[512,4,2,256]{3,1,2,0:T(4,128)(2,1)} %convert_bitcast_fusion.1), kind=kOutput, calls=%fused_computation.49 | convolution fusion | flops 1078198272 | bytes 6291456 | tf_op jit(solution)/shard_map/rk,kszl->rszl/dot_general | solution.py:101
  79.3 5.1 %fusion.45 = f32[512,4,2,256]{3,0,2,1:T(8,128)S(1)} fusion(bf16[512,4,2,256]{3,1,2,0:T(4,128)(2,1)S(1)} %copy-done.6), kind=kOutput, calls=%fused_computation.51 | convolution fusion | flops 1077936128 | bytes 6291456 | tf_op jit(solution)/shard_map/rk,kszl->rszl/dot_general | solution.py:100
  89.3 6.4 %all-to-all-start.1 = ((bf16[8,32,4,256]{3,1,2,0:T(8,128)(2,1)}), bf16[8,32,4,256]{3,1,2,0:T(8,128)(2,1)S(1)}, u32[]{:S(2)}, u32[]{:S(2)}) async-start(bf16[8,32,4,256]{3,1,2,0:T(8,128)(2,1)} %fusion.52), calls=%async_computation.1 | async-start | bytes 1048576 | tf_op jit(solution)/shard_map/all_to_all | solution.py:65
  95.7 13.8 %all-to-all-done.1 = bf16[8,32,4,256]{3,1,2,0:T(8,128)(2,1)S(1)} async-done(((bf16[8,32,4,256]{3,1,2,0:T(8,128)(2,1)}), bf16[8,32,4,256]{3,1,2,0:T(8,128)(2,1)S(1)}, u32[]{:S(2)}, u32[]{:S(2)}) %all-to-all-start.1) | async-done | bytes 524320 | tf_op jit(solution)/shard_map/all_to_all | solution.py:65
  109.6 4.6 %collective-permute-start.1 = (f32[3,4,256]{2,0,1:T(4,128)S(1)}, f32[3,4,256]{2,0,1:T(4,128)S(1)}, u32[]{:S(2)}, u32[]{:S(2)}) collective-permute-start(f32[3,4,256]{2,0,1:T(4,128)S(1)} %get-tuple-element.25), channel_id=1, source_target_pairs={{0,1},{1,2},{2,3},{3,4},{4,5},{5,6},{6,7},{7,8},{8,9},{9,10},{10,1... | collective-permute-start | bytes 36872 | tf_op jit(solution)/shard_map/ppermute | solution.py:19
  116.2 3.1 %collective-permute-done.2 = f32[3,4,256]{2,0,1:T(4,128)S(1)} collective-permute-done((f32[3,4,256]{2,0,1:T(4,128)S(1)}, f32[3,4,256]{2,0,1:T(4,128)S(1)}, u32[]{:S(2)}, u32[]{:S(2)}) %collective-permute-start.2) | collective-permute-done | bytes 12320 | tf_op jit(solution)/shard_map/ppermute | solution.py:21
  119.8 4.7 %collective-permute-done.3 = bf16[32,4,256]{2,0,1:T(8,128)(2,1)S(1)} collective-permute-done((bf16[32,4,256]{2,0,1:T(8,128)(2,1)S(1)}, bf16[32,4,256]{2,0,1:T(8,128)(2,1)S(1)}, u32[]{:S(2)}, u32[]{:S(2)}) %collective-permute-start.3) | collective-permute-done | bytes 65568 | tf_op jit(solution)/shard_map/ppermute | solution.py:42
  124.7 4.9 %collective-permute-done.4 = bf16[2,32,4,256]{3,1,0,2:T(8,128)(2,1)S(1)} collective-permute-done((bf16[2,32,4,256]{3,1,0,2:T(8,128)(2,1)S(1)}, bf16[2,32,4,256]{3,1,0,2:T(8,128)(2,1)S(1)}, u32[]{:S(2)}, u32[]{:S(2)}) %collective-permute-start.4) | collective-permute-done | bytes 131104 | tf_op jit(solution)/shard_map/ppermute | solution.py:42
  130.8 6.1 %collective-permute-done.5 = bf16[2,2,32,4,256]{4,2,1,0,3:T(8,128)(2,1)S(1)} collective-permute-done((bf16[2,2,32,4,256]{4,2,1,0,3:T(8,128)(2,1)S(1)}, bf16[2,2,32,4,256]{4,2,1,0,3:T(8,128)(2,1)S(1)}, u32[]{:S(2)}, u32[]{:S(2)}) %collective-permute-start.5) | collective-permute-done | bytes 262176 | tf_op jit(solution)/shard_map/ppermute | solution.py:42
  143.0 6.7 %fusion.39 = f32[512,4,2,256]{3,0,2,1:T(8,128)S(1)} fusion(bf16[4,512,2,256]{3,2,1,0:T(2,128)(2,1)} %reshape.79), kind=kOutput, calls=%fused_computation.45 | convolution fusion | flops 1078198272 | bytes 6291456 | tf_op jit(solution)/shard_map/kr,srzl->kszl/dot_general | solution.py:171
  149.7 4.9 %fusion.41 = f32[512,4,2,256]{3,0,2,1:T(8,128)S(1)} fusion(bf16[4,512,2,256]{3,2,1,0:T(2,128)(2,1)S(1)} %copy-done), kind=kOutput, calls=%fused_computation.47 | convolution fusion | flops 1077936128 | bytes 6291456 | tf_op jit(solution)/shard_map/kr,srzl->kszl/dot_general | solution.py:170
  155.8 21.2 %convert_bitcast_fusion = bf16[512,4,2,256]{3,1,2,0:T(4,128)(2,1)} fusion(f32[512,32,256]{2,1,0:T(8,128)} %convert_element_type.140, bf16[512,32,2,256]{3,2,1,0:T(2,128)(2,1)} %param.6, bf16[512,4,2,256]{3,0,2,1:T(8,128)(2,1)S(1)} %pad_maximum_fusion.1, f32[32,4]{0,1:T(4,128)S(1)} %copy-done.3, f32[32]{0:T(128)S(1)} %convert_multiply_fusion.1), kind=kOutput, calls=%fused_computation.39 | convolution fusion | flops 176160896 | bytes 37749376 | tf_op jit(solution)/shard_map/cs,kczl->kszl/dot_general | solution.py:117
  177.0 6.9 %fusion.35 = f32[512,4,2,256]{3,0,2,1:T(8,128)S(1)} fusion(bf16[512,4,2,256]{3,1,2,0:T(4,128)(2,1)} %convert_bitcast_fusion), kind=kOutput, calls=%fused_computation.41 | convolution fusion | flops 1078198272 | bytes 6291456 | tf_op jit(solution)/shard_map/rk,kszl->rszl/dot_general | solution.py:101
  183.9 5.1 %fusion.37 = f32[512,4,2,256]{3,0,2,1:T(8,128)S(1)} fusion(bf16[512,4,2,256]{3,1,2,0:T(4,128)(2,1)S(1)} %copy-done.5), kind=kOutput, calls=%fused_computation.43 | convolution fusion | flops 1077936128 | bytes 6291456 | tf_op jit(solution)/shard_map/rk,kszl->rszl/dot_general | solution.py:100
  193.0 17.2 %all_to_all.15 = bf16[8,32,4,256]{3,1,2,0:T(8,128)(2,1)S(1)} all-to-all(bf16[8,32,4,256]{3,1,2,0:T(8,128)(2,1)S(1)} %fusion.53), channel_id=1, replica_groups={{0,2,4,6,8,10,12,14},{1,3,5,7,9,11,13,15},{16,18,20,22,24,26,28,30},{17..., dimensions={0} | all-to-all | bytes 1048576 | tf_op jit(solution)/shard_map/all_to_all | solution.py:65
  210.3 4.7 %collective-permute-start.8 = (f32[3,4,256]{2,0,1:T(4,128)S(1)}, f32[3,4,256]{2,0,1:T(4,128)S(1)}, u32[]{:S(2)}, u32[]{:S(2)}) collective-permute-start(f32[3,4,256]{2,0,1:T(4,128)S(1)} %get-tuple-element.21), channel_id=1, source_target_pairs={{0,1},{1,2},{2,3},{3,4},{4,5},{5,6},{6,7},{7,8},{8,9},{9,10},{10,1... | collective-permute-start | bytes 36872 | tf_op jit(solution)/shard_map/ppermute | solution.py:19
  217.0 3.1 %collective-permute-done.9 = f32[3,4,256]{2,0,1:T(4,128)S(1)} collective-permute-done((f32[3,4,256]{2,0,1:T(4,128)S(1)}, f32[3,4,256]{2,0,1:T(4,128)S(1)}, u32[]{:S(2)}, u32[]{:S(2)}) %collective-permute-start.9) | collective-permute-done | bytes 12320 | tf_op jit(solution)/shard_map/ppermute | solution.py:21
  (77 shorter events, 31.7 us)
Async XLA Ops:
  2.1 30.5 %all-to-all-start = ((bf16[16,32,4,256]{3,1,2,0:T(8,128)(2,1)}), bf16[16,32,4,256]{3,1,2,0:T(8,128)(2,1)S(1)}, u32[]{:S(2)}, u32[]{:S(2)}) async-start(bf16[16,32,4,256]{3,1,2,0:T(8,128)(2,1)} %broadcast_in_dim.43), calls=%async_computation | async-start | bytes 2097152 | tf_op jit(solution)/shard_map/all_to_all | solution.py:31
  9.4 12.4 %copy-start.4 = (s32[32]{0:T(128)S(1)}, s32[32]{0:T(128)}, u32[]{:S(2)}) copy-start(s32[32]{0:T(128)} %param.9) | copy-start | bytes 388
  50.0 0.7 copy-start.3
  72.4 6.9 %copy-start.6 = (bf16[512,4,2,256]{3,1,2,0:T(4,128)(2,1)S(1)}, bf16[512,4,2,256]{3,1,2,0:T(4,128)(2,1)}, u32[]{:S(2)}) copy-start(bf16[512,4,2,256]{3,1,2,0:T(4,128)(2,1)} %convert_bitcast_fusion.1) | copy-start | bytes 6291460
  86.2 9.5 %copy-start.2 = (s32[4,2]{0,1:T(2,128)S(1)}, s32[4,2]{0,1:T(2,128)}, u32[]{:S(2)}) copy-start(s32[4,2]{0,1:T(2,128)} %param.10) | copy-start | bytes 100
  86.2 23.4 %copy-start.1 = (f32[32,4,256]{2,1,0:T(4,128)S(1)}, f32[32,4,256]{2,1,0:T(4,128)}, u32[]{:S(2)}) copy-start(f32[32,4,256]{2,1,0:T(4,128)} %param.11) | copy-start | bytes 393220
  86.2 2.0 collective-permute-start
  89.3 20.2 %all-to-all-start.1 = ((bf16[8,32,4,256]{3,1,2,0:T(8,128)(2,1)}), bf16[8,32,4,256]{3,1,2,0:T(8,128)(2,1)S(1)}, u32[]{:S(2)}, u32[]{:S(2)}) async-start(bf16[8,32,4,256]{3,1,2,0:T(8,128)(2,1)} %fusion.52), calls=%async_computation.1 | async-start | bytes 1048576 | tf_op jit(solution)/shard_map/all_to_all | solution.py:65
  109.6 6.6 %collective-permute-start.1 = (f32[3,4,256]{2,0,1:T(4,128)S(1)}, f32[3,4,256]{2,0,1:T(4,128)S(1)}, u32[]{:S(2)}, u32[]{:S(2)}) collective-permute-start(f32[3,4,256]{2,0,1:T(4,128)S(1)} %get-tuple-element.25), channel_id=1, source_target_pairs={{0,1},{1,2},{2,3},{3,4},{4,5},{5,6},{6,7},{7,8},{8,9},{9,10},{10,1... | collective-permute-start | bytes 36872 | tf_op jit(solution)/shard_map/ppermute | solution.py:19
  114.2 5.1 %collective-permute-start.2 = (f32[3,4,256]{2,0,1:T(4,128)S(1)}, f32[3,4,256]{2,0,1:T(4,128)S(1)}, u32[]{:S(2)}, u32[]{:S(2)}) collective-permute-start(f32[3,4,256]{2,0,1:T(4,128)S(1)} %get-tuple-element.26), channel_id=1, source_target_pairs={{1,0},{2,1},{3,2},{4,3},{5,4},{6,5},{7,6},{8,7},{9,8},{10,9},{11,1... | collective-permute-start | bytes 36872 | tf_op jit(solution)/shard_map/ppermute | solution.py:21
  119.8 4.8 %collective-permute-start.3 = (bf16[32,4,256]{2,0,1:T(8,128)(2,1)S(1)}, bf16[32,4,256]{2,0,1:T(8,128)(2,1)S(1)}, u32[]{:S(2)}, u32[]{:S(2)}) collective-permute-start(bf16[32,4,256]{2,0,1:T(8,128)(2,1)S(1)} %get-tuple-element.5), channel_id=1, source_target_pairs={{0,8},{1,9},{2,10},{3,11},{4,12},{5,13},{6,14},{7,15},{8,0},{9,1},... | collective-permute-start | bytes 196616 | tf_op jit(solution)/shard_map/ppermute | solution.py:42
  124.6 5.0 %collective-permute-start.4 = (bf16[2,32,4,256]{3,1,0,2:T(8,128)(2,1)S(1)}, bf16[2,32,4,256]{3,1,0,2:T(8,128)(2,1)S(1)}, u32[]{:S(2)}, u32[]{:S(2)}) collective-permute-start(bf16[2,32,4,256]{3,1,0,2:T(8,128)(2,1)S(1)} %pad_maximum_fusion.15), channel_id=1, source_target_pairs={{0,4},{1,5},{2,6},{3,7},{4,0},{5,1},{6,2},{7,3},{8,12},{9,13},{10,... | collective-permute-start | bytes 393224 | tf_op jit(solution)/shard_map/ppermute | solution.py:42
  129.6 7.3 %collective-permute-start.5 = (bf16[2,2,32,4,256]{4,2,1,0,3:T(8,128)(2,1)S(1)}, bf16[2,2,32,4,256]{4,2,1,0,3:T(8,128)(2,1)S(1)}, u32[]{:S(2)}, u32[]{:S(2)}) collective-permute-start(bf16[2,2,32,4,256]{4,2,1,0,3:T(8,128)(2,1)S(1)} %pad_maximum_fusion.8), channel_id=1, source_target_pairs={{0,2},{1,3},{2,0},{3,1},{4,6},{5,7},{6,4},{7,5},{8,10},{9,11},{10,... | collective-permute-start | bytes 786440 | tf_op jit(solution)/shard_map/ppermute | solution.py:42
  137.0 3.1 %collective-permute-start.6 = (bf16[2,2,2,32,4,256]{5,3,2,1,0,4:T(8,128)(2,1)S(1)}, bf16[2,2,2,32,4,256]{5,3,2,1,0,4:T(8,128)(2,1)S(1)}, u32[]{:S(2)}, u32[]{:S(2)}) collective-permute-start(bf16[2,2,2,32,4,256]{5,3,2,1,0,4:T(8,128)(2,1)S(1)} %pad_maximum_fusion.5), channel_id=1, source_target_pairs={{0,1},{1,0},{2,3},{3,2},{4,5},{5,4},{6,7},{7,6},{8,9},{9,8},{10,11... | collective-permute-start | bytes 1572872 | tf_op jit(solution)/shard_map/ppermute | solution.py:42
  143.0 6.7 %copy-start = (bf16[4,512,2,256]{3,2,1,0:T(2,128)(2,1)S(1)}, bf16[4,512,2,256]{3,2,1,0:T(2,128)(2,1)}, u32[]{:S(2)}) copy-start(bf16[4,512,2,256]{3,2,1,0:T(2,128)(2,1)} %reshape.79) | copy-start | bytes 6291460
  177.0 6.9 %copy-start.5 = (bf16[512,4,2,256]{3,1,2,0:T(4,128)(2,1)S(1)}, bf16[512,4,2,256]{3,1,2,0:T(4,128)(2,1)}, u32[]{:S(2)}) copy-start(bf16[512,4,2,256]{3,1,2,0:T(4,128)(2,1)} %convert_bitcast_fusion) | copy-start | bytes 6291460
  190.7 2.0 collective-permute-start.7
  210.3 6.7 %collective-permute-start.8 = (f32[3,4,256]{2,0,1:T(4,128)S(1)}, f32[3,4,256]{2,0,1:T(4,128)S(1)}, u32[]{:S(2)}, u32[]{:S(2)}) collective-permute-start(f32[3,4,256]{2,0,1:T(4,128)S(1)} %get-tuple-element.21), channel_id=1, source_target_pairs={{0,1},{1,2},{2,3},{3,4},{4,5},{5,6},{6,7},{7,8},{8,9},{9,10},{10,1... | collective-permute-start | bytes 36872 | tf_op jit(solution)/shard_map/ppermute | solution.py:19
  215.0 5.1 %collective-permute-start.9 = (f32[3,4,256]{2,0,1:T(4,128)S(1)}, f32[3,4,256]{2,0,1:T(4,128)S(1)}, u32[]{:S(2)}, u32[]{:S(2)}) collective-permute-start(f32[3,4,256]{2,0,1:T(4,128)S(1)} %get-tuple-element.22), channel_id=1, source_target_pairs={{1,0},{2,1},{3,2},{4,3},{5,4},{6,5},{7,6},{8,7},{9,8},{10,9},{11,1... | collective-permute-start | bytes 36872 | tf_op jit(solution)/shard_map/ppermute | solution.py:21
